TPU v7x, 256 devices: a whole 4x4x8 slice. The times are simulated.
256 devices in a mesh: blk: 4 (over x), shard: 64 (over y, z, core).
Axes of the slice: x: 4, y: 4, z: 8, core: 2. Of those that a mesh axis runs over, the one named last changes fastest.
Arguments:
- table: bfloat16 [524288, 400], P(('blk', 'shard')), may hold values from -3 to 3
- relation: bfloat16 [1345, 400], replicated, may hold values from -3 to 3
- owners: int32 [262144, 2], P(('blk', 'shard')), may hold values from 0 to 63, all different within a row; in each aligned block of 1024 rows (0 to 1023, 1024 to 2047, ...) at most 64 rows name the same one
- rows: int32 [262144, 2], P(('blk', 'shard')), may hold values from 0 to 2047
- rel_ids: int32 [262144], P(('blk', 'shard')), may hold values from 0 to 1344
- span_ids: int32 [256], P(('blk', 'shard')), may hold values from 0 to 1
Outputs:
- entity_grad: float32 [524288, 400], P(('blk', 'shard'))
- relation_grad: float32 [1345, 400], replicated
Inputs may be any that keep to these rules, and one draw needn't show every extreme that they name: Among the 1024 edges of one device no owner index is named by more than 64 edge ends; an edge's source and target owners differ; ends address rows of the devices with the same blk index.
All inputs are finite; a program needn't handle non-finite values.
Results may differ from a plain program's by a relative error of at most 0.0016.
Values may be sent and summed in bfloat16 or wider, within the bound.
No kernel may reach another device: no remote copies, remote signals or barrier semaphores. Data moves between devices by JAX's collectives and lax.ppermute only.
A program may use at most 128 MiB of HBM per device.

v0:
```python
import math
import jax
import jax.numpy as jnp
from jax import lax
from jax.sharding import PartitionSpec as P

NEG = 1024


def from_behind(value, axis, by):
    length = lax.axis_size(axis)
    return lax.ppermute(value, axis, [(i, (i + by) % length) for i in range(length)])


def score_span(query_bf, span, weight):
    neg_score = lax.dot_general(
        query_bf, span, (((1,), (1,)), ((), ())), preferred_element_type=jnp.float32
    )
    neg_grad = (weight * jax.nn.sigmoid(neg_score)).astype(jnp.bfloat16)
    query_part = jnp.dot(neg_grad, span, preferred_element_type=jnp.float32)
    span_part = lax.dot_general(
        neg_grad, query_bf, (((0,), (0,)), ((), ())), preferred_element_type=jnp.float32
    )
    return (query_part, span_part)


def shards(table, relation, owners, rows, rel_ids, span_ids):
    n_shard = lax.axis_size("shard")
    n_blk = lax.axis_size("blk")
    edges = owners.shape[0]
    rows_own = table.shape[0]
    width = table.shape[1]
    half = width // 2
    capacity = 4 * edges // n_shard
    negatives = NEG
    flat_owner = owners.reshape(-1)
    flat_row = rows.reshape(-1)
    onehot = (flat_owner[:, None] == jnp.arange(n_shard, dtype=jnp.int32)[None, :]).astype(
        jnp.int32
    )
    ranking = jnp.sum(jnp.cumsum(onehot, axis=0) * onehot, axis=1) - 1
    slots = flat_owner * capacity + ranking
    requests = (
        jnp.zeros((n_shard * capacity,), jnp.int32)
        .at[slots]
        .set(flat_row)
        .reshape(n_shard, capacity)
    )
    asked_rows = lax.all_to_all(requests, "shard", split_axis=0, concat_axis=0, tiled=True)
    fetched = lax.all_to_all(table[asked_rows], "shard", split_axis=0, concat_axis=0, tiled=True)
    gotten = fetched.reshape(n_shard * capacity, width)[slots].reshape(edges, 2, width)
    source = gotten[:, 0].astype(jnp.float32)
    target = gotten[:, 1].astype(jnp.float32)
    rel_rows = relation[rel_ids].astype(jnp.float32)
    s_re, s_im = (source[:, :half], source[:, half:])
    r_re, r_im = (rel_rows[:, :half], rel_rows[:, half:])
    query = jnp.concatenate([s_re * r_re - s_im * r_im, s_re * r_im + s_im * r_re], axis=1)
    pos_grad = jax.nn.sigmoid(jnp.sum(query * target, axis=1)) - 1.0
    query_bf = query.astype(jnp.bfloat16)
    weight = 1.0 / math.sqrt(n_blk * negatives)
    span_start = span_ids[0] * negatives
    span = lax.dynamic_slice_in_dim(table, span_start, negatives, 0)
    query_grad = pos_grad[:, None] * target
    carried = jnp.zeros((negatives, width), jnp.float32)
    for visit in range(n_blk):
        query_part, span_part = score_span(query_bf, span, weight)
        query_grad = query_grad + query_part
        carried = carried + span_part
        if visit + 1 < n_blk:
            span = from_behind(span, "blk", 1)
        carried = from_behind(carried, "blk", 1)
    q_re, q_im = (query_grad[:, :half], query_grad[:, half:])
    source_grad = jnp.concatenate([q_re * r_re + q_im * r_im, q_im * r_re - q_re * r_im], axis=1)
    rel_term = jnp.concatenate([q_re * s_re + q_im * s_im, q_im * s_re - q_re * s_im], axis=1)
    target_grad = pos_grad[:, None] * query
    local_relation = jnp.zeros((relation.shape[0], width), jnp.float32).at[rel_ids].add(rel_term)
    relation_grad = lax.psum(local_relation, ("blk", "shard"))
    end_grads = jnp.stack([source_grad, target_grad], axis=1).reshape(2 * edges, width)
    outgoing = jnp.zeros((n_shard * capacity, width), jnp.float32).at[slots].set(end_grads)
    arrived = lax.all_to_all(
        outgoing.reshape(n_shard, capacity, width), "shard", split_axis=0, concat_axis=0, tiled=True
    )
    entity_grad = (
        jnp.zeros((rows_own, width), jnp.float32)
        .at[asked_rows.reshape(-1)]
        .add(arrived.reshape(-1, width))
    )
    current = lax.dynamic_slice_in_dim(entity_grad, span_start, negatives, 0)
    entity_grad = lax.dynamic_update_slice_in_dim(entity_grad, current + carried, span_start, 0)
    return (entity_grad, relation_grad)


def solution(mesh):
    in_specs = (
        P(("blk", "shard"), None),
        P(),
        P(("blk", "shard"), None),
        P(("blk", "shard"), None),
        P(("blk", "shard")),
        P(("blk", "shard")),
    )
    out_specs = (P(("blk", "shard"), None), P())
    return jax.shard_map(shards, mesh=mesh, in_specs=in_specs, out_specs=out_specs, check_vma=False)
```

profile of v0, /device:TPU:16, one launch (start us, length us, event | category | flops | bytes accessed | tf_op | source)
XLA Modules:
  0.0 731.5 jit_solution(13740159022034079875)
XLA Ops:
  9.9 18.1 %reduce-window.6 = s32[64,16,128]{2,1,0:T(8,128)S(1)} reduce-window(s32[64,16,128]{2,1,0:T(8,128)S(1)} %fusion.14, s32[]{:T(128)} %constant.12.clone.1), window={size=1x1x128 pad=0_0x0_0x127_0}, to_apply=%region_0.0 | reduce-window | flops 16646144 | bytes 1048580 | tf_op jit(solution)/shard_map/reduce-window
  29.9 8.1 %scatter_custom_fusion = s32[4096]{0:T(1024)S(1)} fusion(s32[2048]{0:T(1024)S(1)} %bitcast.72, s32[2048]{0:T(1024)S(1)} %reshape.235, s32[]{:T(128)} %constant.12.clone.1), kind=kCustom, calls=%fused_computation.50 | custom fusion | bytes 16388 | tf_op jit(solution)/shard_map/scatter | solution.py:46
  38.6 12.1 %all-to-all-start = ((s32[64,1,64]{2,1,0:T(1,128)}), s32[64,1,64]{2,1,0:T(1,128)S(1)}, u32[]{:S(2)}, u32[]{:S(2)}) async-start(s32[64,1,64]{2,1,0:T(1,128)} %all_to_all.14), calls=%async_computation | async-start | bytes 65536 | tf_op jit(solution)/shard_map/all_to_all | solution.py:49
  53.5 4.8 all-to-all-done
  58.4 17.3 %gather_fusion = bf16[4096,400]{1,0:T(8,128)(2,1)} fusion(bf16[2048,400]{1,0:T(8,128)(2,1)S(1)} %copy.17, s32[4096]{0:T(1024)S(1)} %broadcast_clamp_fusion), kind=kCustom, calls=%fused_computation | custom fusion | bytes 6569984 | tf_op jit(solution)/shard_map/gather | solution.py:50
  75.7 7.5 %all-to-all-start.1 = ((bf16[64,64,400]{2,1,0:T(8,128)(2,1)}), bf16[64,64,400]{2,1,0:T(8,128)(2,1)}, u32[]{:S(2)}, u32[]{:S(2)}) async-start(bf16[64,64,400]{2,1,0:T(8,128)(2,1)} %bitcast.65), calls=%async_computation.1 | async-start | bytes 8388608 | tf_op jit(solution)/shard_map/all_to_all | solution.py:50
  85.7 20.1 %collective-permute-done = bf16[1024,400]{0,1:T(8,128)(2,1)} collective-permute-done((bf16[1024,400]{0,1:T(8,128)(2,1)S(1)}, bf16[1024,400]{0,1:T(8,128)(2,1)}, u32[]{:S(2)}, u32[]{:S(2)}) %collective-permute-start) | collective-permute-done | bytes 819232 | tf_op jit(solution)/shard_map/ppermute | solution.py:12
  112.8 14.0 %collective-permute-done.1 = bf16[1024,400]{0,1:T(8,128)(2,1)} collective-permute-done((bf16[1024,400]{0,1:T(8,128)(2,1)}, bf16[1024,400]{0,1:T(8,128)(2,1)}, u32[]{:S(2)}, u32[]{:S(2)}) %collective-permute-start.1) | collective-permute-done | bytes 819232 | tf_op jit(solution)/shard_map/ppermute | solution.py:12
  126.8 49.3 %all-to-all-done.1 = bf16[64,64,400]{2,1,0:T(8,128)(2,1)} async-done(((bf16[64,64,400]{2,1,0:T(8,128)(2,1)}), bf16[64,64,400]{2,1,0:T(8,128)(2,1)}, u32[]{:S(2)}, u32[]{:S(2)}) %all-to-all-start.1) | async-done | bytes 3276832 | tf_op jit(solution)/shard_map/all_to_all | solution.py:50
  176.1 12.0 %gather_fusion.1 = bf16[2048,400]{1,0:T(8,128)(2,1)} fusion(bf16[4096,400]{1,0:T(8,128)(2,1)} %bitcast.8, s32[2048]{0:T(1024)S(1)} %broadcast_clamp_fusion.1), kind=kCustom, calls=%fused_computation.1 | custom fusion | bytes 3284992 | tf_op jit(solution)/shard_map/gather | solution.py:51
  190.9 4.2 fusion.17
  195.1 4.6 copy.30
  199.8 4.9 copy.29
  230.8 4.6 copy.22
  235.4 6.2 reshape.243
  241.6 13.4 %scatter_custom_fusion.1 = f32[4096,400]{1,0:T(8,128)} fusion(s32[2048]{0:T(1024)S(1)} %bitcast.74, f32[2048,400]{1,0:T(8,128)} %reshape.243, f32[]{:T(128)} %constant.11.clone.1), kind=kCustom, calls=%fused_computation.11 | custom fusion | bytes 6554112 | tf_op jit(solution)/shard_map/scatter | solution.py:79
  255.0 9.2 %all-to-all-start.2 = ((f32[64,64,400]{2,1,0:T(8,128)}), f32[64,64,400]{2,1,0:T(8,128)}, u32[]{:S(2)}, u32[]{:S(2)}) async-start(f32[64,64,400]{2,1,0:T(8,128)} %bitcast.64), calls=%async_computation.2 | async-start | bytes 16777216 | tf_op jit(solution)/shard_map/all_to_all | solution.py:80
  266.9 37.6 %collective-permute-done.3 = f32[1024,400]{0,1:T(8,128)S(1)} collective-permute-done((f32[1024,400]{0,1:T(8,128)S(1)}, f32[1024,400]{0,1:T(8,128)S(1)}, u32[]{:S(2)}, u32[]{:S(2)}) %collective-permute-start.3) | collective-permute-done | bytes 1638432 | tf_op jit(solution)/shard_map/ppermute | solution.py:12
  306.9 37.0 %collective-permute-done.4 = f32[1024,400]{0,1:T(8,128)S(1)} collective-permute-done((f32[1024,400]{0,1:T(8,128)S(1)}, f32[1024,400]{0,1:T(8,128)S(1)}, u32[]{:S(2)}, u32[]{:S(2)}) %collective-permute-start.4) | collective-permute-done | bytes 1638432 | tf_op jit(solution)/shard_map/ppermute | solution.py:12
  345.5 36.4 %collective-permute-done.5 = f32[1024,400]{0,1:T(8,128)S(1)} collective-permute-done((f32[1024,400]{0,1:T(8,128)S(1)}, f32[1024,400]{0,1:T(8,128)S(1)}, u32[]{:S(2)}, u32[]{:S(2)}) %collective-permute-start.5) | collective-permute-done | bytes 1638432 | tf_op jit(solution)/shard_map/ppermute | solution.py:12
  385.6 8.9 %scatter_custom_fusion.3 = f32[1345,400]{1,0:T(8,128)} fusion(s32[1024]{0:T(1024)S(1)} %get-tuple-element.14, f32[1024,400]{1,0:T(8,128)} %copy.25, f32[]{:T(128)} %constant.11.clone.1), kind=kCustom, calls=%fused_computation.28 | custom fusion | flops 409600 | bytes 2152512 | tf_op jit(solution)/shard_map/scatter-add | solution.py:76
  395.9 279.5 %all-reduce.2.cloned.1.call-done = f32[1345,400]{1,0:T(8,128)} async-done(((f32[1345,400]{1,0:T(8,128)}), f32[1345,400]{1,0:T(8,128)}) %all-reduce.2.cloned.1.call-update) | async-done | bytes 2152016 | tf_op jit(solution)/shard_map/psum | solution.py:77
  678.7 30.1 %scatter_custom_fusion.2 = f32[2048,400]{1,0:T(8,128)} fusion(s32[4096]{0:T(1024)S(1)} %bitcast.76, f32[4096,400]{1,0:T(8,128)} %bitcast.17, f32[]{:T(128)} %constant.11.clone.1), kind=kCustom, calls=%fused_computation.14 | custom fusion | flops 1638400 | bytes 3277312 | tf_op jit(solution)/shard_map/scatter-add | solution.py:86
  719.0 5.2 copy.26
  (114 shorter events, 70.4 us)
Async XLA Ops:
  9.9 19.4 %copy-start.11 = (s32[1024,2]{0,1:T(2,128)S(1)}, s32[1024,2]{0,1:T(2,128)}, u32[]{:S(2)}) copy-start(s32[1024,2]{0,1:T(2,128)} %param.9) | copy-start | bytes 24580
  38.6 19.7 %all-to-all-start = ((s32[64,1,64]{2,1,0:T(1,128)}), s32[64,1,64]{2,1,0:T(1,128)S(1)}, u32[]{:S(2)}, u32[]{:S(2)}) async-start(s32[64,1,64]{2,1,0:T(1,128)} %all_to_all.14), calls=%async_computation | async-start | bytes 65536 | tf_op jit(solution)/shard_map/all_to_all | solution.py:49
  75.7 8.3 %copy-start.1 = (bf16[2048,400]{0,1:T(8,128)(2,1)S(1)}, bf16[2048,400]{0,1:T(8,128)(2,1)}, u32[]{:S(2)}) copy-start(bf16[2048,400]{0,1:T(8,128)(2,1)} %param.6) | copy-start | bytes 4915204
  75.7 100.4 %all-to-all-start.1 = ((bf16[64,64,400]{2,1,0:T(8,128)(2,1)}), bf16[64,64,400]{2,1,0:T(8,128)(2,1)}, u32[]{:S(2)}, u32[]{:S(2)}) async-start(bf16[64,64,400]{2,1,0:T(8,128)(2,1)} %bitcast.65), calls=%async_computation.1 | async-start | bytes 8388608 | tf_op jit(solution)/shard_map/all_to_all | solution.py:50
  83.2 22.8 %copy-start.6 = (bf16[1345,400]{0,1:T(8,128)(2,1)S(1)}, bf16[1345,400]{0,1:T(8,128)(2,1)}, u32[]{:S(2)}) copy-start(bf16[1345,400]{0,1:T(8,128)(2,1)} %param.7) | copy-start | bytes 3228004
  83.3 23.7 %copy-start.12 = (s32[1024]{0:T(1024)S(1)}, s32[1024]{0:T(1024)}, u32[]{:S(2)}) copy-start(s32[1024]{0:T(1024)} %param.10) | copy-start | bytes 12292
  84.1 21.7 %copy-start.9 = (bf16[1024,400]{0,1:T(8,128)(2,1)}, bf16[1024,400]{0,1:T(8,128)(2,1)S(1)}, u32[]{:S(2)}) copy-start(bf16[1024,400]{0,1:T(8,128)(2,1)S(1)} %constant_dynamic-slice_fusion.1) | copy-start | bytes 2457604
  84.1 21.7 %collective-permute-start = (bf16[1024,400]{0,1:T(8,128)(2,1)S(1)}, bf16[1024,400]{0,1:T(8,128)(2,1)}, u32[]{:S(2)}, u32[]{:S(2)}) collective-permute-start(bf16[1024,400]{0,1:T(8,128)(2,1)S(1)} %constant_dynamic-slice_fusion.1), channel_id=1, source_target_pairs={{0,64},{64,128},{128,192},{192,0},{1,65},{65,129},{129,193},{193,1... | collective-permute-start | bytes 2457608 | tf_op jit(solution)/shard_map/ppermute | solution.py:12
  105.8 21.0 %collective-permute-start.1 = (bf16[1024,400]{0,1:T(8,128)(2,1)}, bf16[1024,400]{0,1:T(8,128)(2,1)}, u32[]{:S(2)}, u32[]{:S(2)}) collective-permute-start(bf16[1024,400]{0,1:T(8,128)(2,1)} %collective-permute-done), channel_id=1, source_target_pairs={{0,64},{64,128},{128,192},{192,0},{1,65},{65,129},{129,193},{193,1... | collective-permute-start | bytes 2457608 | tf_op jit(solution)/shard_map/ppermute | solution.py:12
  126.8 89.9 %collective-permute-start.2 = (bf16[1024,400]{0,1:T(8,128)(2,1)}, bf16[1024,400]{0,1:T(8,128)(2,1)}, u32[]{:S(2)}, u32[]{:S(2)}) collective-permute-start(bf16[1024,400]{0,1:T(8,128)(2,1)} %collective-permute-done.1), channel_id=1, source_target_pairs={{0,64},{64,128},{128,192},{192,0},{1,65},{65,129},{129,193},{193,1... | collective-permute-start | bytes 2457608 | tf_op jit(solution)/shard_map/ppermute | solution.py:12
  205.5 11.2 %copy-start.7 = (bf16[1024,400]{0,1:T(8,128)(2,1)}, bf16[1024,400]{0,1:T(8,128)(2,1)S(1)}, u32[]{:S(2)}) copy-start(bf16[1024,400]{0,1:T(8,128)(2,1)S(1)} %fusion.11) | copy-start | bytes 2457604
  255.0 9.3 %copy-start.8 = (bf16[1024,400]{0,1:T(8,128)(2,1)S(1)}, bf16[1024,400]{0,1:T(8,128)(2,1)}, u32[]{:S(2)}) copy-start(bf16[1024,400]{0,1:T(8,128)(2,1)} %copy-done.7) | copy-start | bytes 2457604
  255.0 9.3 %copy-start.18 = (bf16[1024,1024]{1,0:T(8,128)(2,1)S(1)}, bf16[1024,1024]{1,0:T(8,128)(2,1)}, u32[]{:S(2)}) copy-start(bf16[1024,1024]{1,0:T(8,128)(2,1)} %copy-done.17) | copy-start | bytes 6291460
  255.0 423.6 %all-to-all-start.2 = ((f32[64,64,400]{2,1,0:T(8,128)}), f32[64,64,400]{2,1,0:T(8,128)}, u32[]{:S(2)}, u32[]{:S(2)}) async-start(f32[64,64,400]{2,1,0:T(8,128)} %bitcast.64), calls=%async_computation.2 | async-start | bytes 16777216 | tf_op jit(solution)/shard_map/all_to_all | solution.py:80
  264.2 411.2 %all-reduce.2.cloned.1.call-start = ((), (), s32[]{:S(2)}) async-start(), calls=%async_computation.3 | async-start | bytes 5537792 | tf_op jit(solution)/shard_map/psum | solution.py:77
  264.3 40.2 %copy-start.14 = (bf16[1024,1024]{1,0:T(8,128)(2,1)S(1)}, bf16[1024,1024]{1,0:T(8,128)(2,1)}, u32[]{:S(2)}) copy-start(bf16[1024,1024]{1,0:T(8,128)(2,1)} %copy-done.13) | copy-start | bytes 6291460
  265.3 40.5 %copy-start.16 = (bf16[1024,1024]{1,0:T(8,128)(2,1)S(1)}, bf16[1024,1024]{1,0:T(8,128)(2,1)}, u32[]{:S(2)}) copy-start(bf16[1024,1024]{1,0:T(8,128)(2,1)} %copy-done.15) | copy-start | bytes 6291460
  265.4 39.1 %collective-permute-start.3 = (f32[1024,400]{0,1:T(8,128)S(1)}, f32[1024,400]{0,1:T(8,128)S(1)}, u32[]{:S(2)}, u32[]{:S(2)}) collective-permute-start(f32[1024,400]{0,1:T(8,128)S(1)} %fusion.21), channel_id=1, source_target_pairs={{0,64},{64,128},{128,192},{192,0},{1,65},{65,129},{129,193},{193,1... | collective-permute-start | bytes 4915208 | tf_op jit(solution)/shard_map/ppermute | solution.py:12
  305.5 38.4 %collective-permute-start.4 = (f32[1024,400]{0,1:T(8,128)S(1)}, f32[1024,400]{0,1:T(8,128)S(1)}, u32[]{:S(2)}, u32[]{:S(2)}) collective-permute-start(f32[1024,400]{0,1:T(8,128)S(1)} %convolution_add_fusion), channel_id=1, source_target_pairs={{0,64},{64,128},{128,192},{192,0},{1,65},{65,129},{129,193},{193,1... | collective-permute-start | bytes 4915208 | tf_op jit(solution)/shard_map/ppermute | solution.py:12
  306.9 37.5 %copy-start.5 = (bf16[1024,1024]{1,0:T(8,128)(2,1)S(1)}, bf16[1024,1024]{1,0:T(8,128)(2,1)}, u32[]{:S(2)}) copy-start(bf16[1024,1024]{1,0:T(8,128)(2,1)} %copy-done.4) | copy-start | bytes 6291460
  344.3 37.6 %collective-permute-start.5 = (f32[1024,400]{0,1:T(8,128)S(1)}, f32[1024,400]{0,1:T(8,128)S(1)}, u32[]{:S(2)}, u32[]{:S(2)}) collective-permute-start(f32[1024,400]{0,1:T(8,128)S(1)} %add.149), channel_id=1, source_target_pairs={{0,64},{64,128},{128,192},{192,0},{1,65},{65,129},{129,193},{193,1... | collective-permute-start | bytes 4915208 | tf_op jit(solution)/shard_map/ppermute | solution.py:12
  345.5 38.2 %copy-start.2 = (f32[1024,200]{0,1:T(8,128)S(1)}, f32[1024,200]{0,1:T(8,128)}, u32[]{:S(2)}) copy-start(f32[1024,200]{0,1:T(8,128)} %get-tuple-element.4) | copy-start | bytes 2457604
  345.5 38.2 %copy-start.3 = (f32[1024,200]{0,1:T(8,128)S(1)}, f32[1024,200]{0,1:T(8,128)}, u32[]{:S(2)}) copy-start(f32[1024,200]{0,1:T(8,128)} %get-tuple-element.5) | copy-start | bytes 2457604
  383.4 328.8 %collective-permute-start.6 = (f32[1024,400]{0,1:T(8,128)}, f32[1024,400]{0,1:T(8,128)}, u32[]{:S(2)}, u32[]{:S(2)}) collective-permute-start(f32[1024,400]{0,1:T(8,128)} %add.150), channel_id=1, source_target_pairs={{0,64},{64,128},{128,192},{192,0},{1,65},{65,129},{129,193},{193,1... | collective-permute-start | bytes 4915208 | tf_op jit(solution)/shard_map/ppermute | solution.py:12
  (6 other events, 26.8 us)
Sparse Core Ops, SparseCore 0:
  394.6 280.7 all-reduce.1
where the time goes:
time: 741 us; the launch traced here: 731 us
  waiting for transfers between devices  479 us (65%)
  local copies, waits for them, and re-layouts  109 us (15%)
  other arithmetic  70 us (9%)
  starting transfers between devices  32.9 us (4%)
  matrix products  24.7 us (3%)
  between operations  15.8 us (2%)
    psum x1, waiting for transfers between devices, shards(): relation_grad = lax.psum(local_relation, ('blk', 'shard'))  280 us
    ppermute x7, waiting for transfers between devices, from_behind(): lax.ppermute(value, axis, [(i, (i + by) % length) for i in range(length)])  145 us
    all_to_all x1, waiting for transfers between devices, shards(): lax.all_to_all(table[asked_rows], 'shard', split_axis=0, concat_axis=0, t...  49.3 us
    scatter-add x1, other arithmetic, shards(): entity_grad = jnp.zeros((rows_own, width), jnp.float32).at[asked_rows.res...  30.1 us
    unnamed x47, local copies, waits for them, and re-layouts  25.7 us
    another operation x3, other arithmetic  18.5 us
    gather x1, local copies, waits for them, and re-layouts, shards(): table[asked_rows]  17.3 us
  transfers between devices with their start and end apart: 11, of which 8 were waited for; matrix products, arithmetic and copies ran while one was open for 14% of the time, Pallas kernels for 0%

commit v1 on v0

--- a/solution.py
+++ b/solution.py
@@ -74,7 +74,7 @@
     rel_term = jnp.concatenate([q_re * s_re + q_im * s_im, q_im * s_re - q_re * s_im], axis=1)
     target_grad = pos_grad[:, None] * query
     local_relation = jnp.zeros((relation.shape[0], width), jnp.float32).at[rel_ids].add(rel_term)
-    relation_grad = lax.psum(local_relation, ("blk", "shard"))
+    relation_grad = lax.psum(lax.psum(local_relation, "blk"), "shard")
     end_grads = jnp.stack([source_grad, target_grad], axis=1).reshape(2 * edges, width)
     outgoing = jnp.zeros((n_shard * capacity, width), jnp.float32).at[slots].set(end_grads)
     arrived = lax.all_to_all(

time: 741 us -> 694 us (0.937)
  waiting for transfers between devices: 479 us -> 428 us
    psum x1 -> x2, waiting for transfers between devices: 280 us -> 208 us  [shards(): relation_grad = lax.psum(lax.psum(local_relation, 'blk'), 'shard')]
    ppermute x7, waiting for transfers between devices: 145 us -> 166 us  [from_behind(): lax.ppermute(value, axis, [(i, (i + by) % length) for i in range(length)])]
  transfers between devices with their start and end apart: 11 -> 12, of which waited for: 8 -> 9; matrix products, arithmetic and copies ran while one was open for 14% -> 16% of each run, Pallas kernels for 0% -> 0%
where the time goes in v1:
time: 694 us; the launch traced here: 683 us
  waiting for transfers between devices  428 us (62%)
  local copies, waits for them, and re-layouts  109 us (16%)
  other arithmetic  70.1 us (10%)
  starting transfers between devices  32.7 us (5%)
  matrix products  27.6 us (4%)
  between operations  15.8 us (2%)
    psum x2, waiting for transfers between devices, shards(): relation_grad = lax.psum(lax.psum(local_relation, 'blk'), 'shard')  208 us
    ppermute x7, waiting for transfers between devices, from_behind(): lax.ppermute(value, axis, [(i, (i + by) % length) for i in range(length)])  166 us
    all_to_all x1, waiting for transfers between devices, shards(): lax.all_to_all(table[asked_rows], 'shard', split_axis=0, concat_axis=0, t...  49.3 us
    scatter-add x1, other arithmetic, shards(): entity_grad = jnp.zeros((rows_own, width), jnp.float32).at[asked_rows.res...  30.1 us
    unnamed x47, local copies, waits for them, and re-layouts  25.7 us
    another operation x3, other arithmetic  18.5 us
    gather x1, local copies, waits for them, and re-layouts, shards(): table[asked_rows]  17.3 us
  transfers between devices with their start and end apart: 12, of which 9 were waited for; matrix products, arithmetic and copies ran while one was open for 16% of the time, Pallas kernels for 0%

profile of v1, /device:TPU:16, one launch (start us, length us, event | category | flops | bytes accessed | tf_op | source)
XLA Modules:
  0.0 683.4 jit_solution(16505956691028256903)
XLA Ops:
  9.9 18.1 %reduce-window.6 = s32[64,16,128]{2,1,0:T(8,128)S(1)} reduce-window(s32[64,16,128]{2,1,0:T(8,128)S(1)} %fusion.14, s32[]{:T(128)} %constant.12.clone.1), window={size=1x1x128 pad=0_0x0_0x127_0}, to_apply=%region_0.0 | reduce-window | flops 16646144 | bytes 1048580 | tf_op jit(solution)/shard_map/reduce-window
  29.9 8.1 %scatter_custom_fusion = s32[4096]{0:T(1024)S(1)} fusion(s32[2048]{0:T(1024)S(1)} %bitcast.72, s32[2048]{0:T(1024)S(1)} %reshape.235, s32[]{:T(128)} %constant.12.clone.1), kind=kCustom, calls=%fused_computation.50 | custom fusion | bytes 16388 | tf_op jit(solution)/shard_map/scatter | solution.py:46
  38.6 12.1 %all-to-all-start = ((s32[64,1,64]{2,1,0:T(1,128)}), s32[64,1,64]{2,1,0:T(1,128)S(1)}, u32[]{:S(2)}, u32[]{:S(2)}) async-start(s32[64,1,64]{2,1,0:T(1,128)} %all_to_all.14), calls=%async_computation | async-start | bytes 65536 | tf_op jit(solution)/shard_map/all_to_all | solution.py:49
  53.5 4.8 all-to-all-done
  58.4 17.3 %gather_fusion = bf16[4096,400]{1,0:T(8,128)(2,1)} fusion(bf16[2048,400]{1,0:T(8,128)(2,1)S(1)} %copy.17, s32[4096]{0:T(1024)S(1)} %broadcast_clamp_fusion), kind=kCustom, calls=%fused_computation | custom fusion | bytes 6569984 | tf_op jit(solution)/shard_map/gather | solution.py:50
  75.7 7.5 %all-to-all-start.1 = ((bf16[64,64,400]{2,1,0:T(8,128)(2,1)}), bf16[64,64,400]{2,1,0:T(8,128)(2,1)}, u32[]{:S(2)}, u32[]{:S(2)}) async-start(bf16[64,64,400]{2,1,0:T(8,128)(2,1)} %bitcast.65), calls=%async_computation.1 | async-start | bytes 8388608 | tf_op jit(solution)/shard_map/all_to_all | solution.py:50
  85.7 20.1 %collective-permute-done = bf16[1024,400]{0,1:T(8,128)(2,1)} collective-permute-done((bf16[1024,400]{0,1:T(8,128)(2,1)S(1)}, bf16[1024,400]{0,1:T(8,128)(2,1)}, u32[]{:S(2)}, u32[]{:S(2)}) %collective-permute-start) | collective-permute-done | bytes 819232 | tf_op jit(solution)/shard_map/ppermute | solution.py:12
  112.9 13.9 %collective-permute-done.1 = bf16[1024,400]{0,1:T(8,128)(2,1)} collective-permute-done((bf16[1024,400]{0,1:T(8,128)(2,1)}, bf16[1024,400]{0,1:T(8,128)(2,1)}, u32[]{:S(2)}, u32[]{:S(2)}) %collective-permute-start.1) | collective-permute-done | bytes 819232 | tf_op jit(solution)/shard_map/ppermute | solution.py:12
  126.8 49.3 %all-to-all-done.1 = bf16[64,64,400]{2,1,0:T(8,128)(2,1)} async-done(((bf16[64,64,400]{2,1,0:T(8,128)(2,1)}), bf16[64,64,400]{2,1,0:T(8,128)(2,1)}, u32[]{:S(2)}, u32[]{:S(2)}) %all-to-all-start.1) | async-done | bytes 3276832 | tf_op jit(solution)/shard_map/all_to_all | solution.py:50
  176.2 12.0 %gather_fusion.1 = bf16[2048,400]{1,0:T(8,128)(2,1)} fusion(bf16[4096,400]{1,0:T(8,128)(2,1)} %bitcast.8, s32[2048]{0:T(1024)S(1)} %broadcast_clamp_fusion.1), kind=kCustom, calls=%fused_computation.1 | custom fusion | bytes 3284992 | tf_op jit(solution)/shard_map/gather | solution.py:51
  195.1 4.6 copy.30
  199.8 4.9 copy.29
  230.8 4.6 copy.22
  235.4 6.2 reshape.243
  241.6 13.4 %scatter_custom_fusion.1 = f32[4096,400]{1,0:T(8,128)} fusion(s32[2048]{0:T(1024)S(1)} %bitcast.74, f32[2048,400]{1,0:T(8,128)} %reshape.243, f32[]{:T(128)} %constant.11.clone.1), kind=kCustom, calls=%fused_computation.11 | custom fusion | bytes 6554112 | tf_op jit(solution)/shard_map/scatter | solution.py:79
  255.0 9.2 %all-to-all-start.2 = ((f32[64,64,400]{2,1,0:T(8,128)}), f32[64,64,400]{2,1,0:T(8,128)}, u32[]{:S(2)}, u32[]{:S(2)}) async-start(f32[64,64,400]{2,1,0:T(8,128)} %bitcast.64), calls=%async_computation.2 | async-start | bytes 16777216 | tf_op jit(solution)/shard_map/all_to_all | solution.py:80
  266.9 37.6 %collective-permute-done.3 = f32[1024,400]{0,1:T(8,128)S(1)} collective-permute-done((f32[1024,400]{0,1:T(8,128)S(1)}, f32[1024,400]{0,1:T(8,128)S(1)}, u32[]{:S(2)}, u32[]{:S(2)}) %collective-permute-start.3) | collective-permute-done | bytes 1638432 | tf_op jit(solution)/shard_map/ppermute | solution.py:12
  309.3 9.0 %scatter_custom_fusion.3 = f32[1345,400]{1,0:T(8,128)} fusion(s32[1024]{0:T(1024)S(1)} %get-tuple-element.14, f32[1024,400]{1,0:T(8,128)} %copy.25, f32[]{:T(128)} %constant.11.clone.1), kind=kCustom, calls=%fused_computation.28 | custom fusion | flops 409600 | bytes 2152512 | tf_op jit(solution)/shard_map/scatter-add | solution.py:76
  321.0 38.2 %collective-permute-done.4 = f32[1024,400]{0,1:T(8,128)S(1)} collective-permute-done((f32[1024,400]{0,1:T(8,128)}, f32[1024,400]{0,1:T(8,128)S(1)}, u32[]{:S(2)}, u32[]{:S(2)}) %collective-permute-start.4) | collective-permute-done | bytes 1638432 | tf_op jit(solution)/shard_map/ppermute | solution.py:12
  360.5 55.8 %collective-permute-done.5 = f32[1024,400]{0,1:T(8,128)S(1)} collective-permute-done((f32[1024,400]{0,1:T(8,128)S(1)}, f32[1024,400]{0,1:T(8,128)S(1)}, u32[]{:S(2)}, u32[]{:S(2)}) %collective-permute-start.5) | collective-permute-done | bytes 1638432 | tf_op jit(solution)/shard_map/ppermute | solution.py:12
  417.8 14.1 %all-reduce.3.cloned.1.call-done = f32[1345,400]{1,0:T(8,128)} async-done(((f32[1345,400]{1,0:T(8,128)}), f32[1345,400]{1,0:T(8,128)}) %all-reduce.3.cloned.1.call-update) | async-done | bytes 2152016 | tf_op jit(solution)/shard_map/psum | solution.py:77
  433.3 194.1 %all-reduce.5.cloned.1.call-done = f32[1345,400]{1,0:T(8,128)} async-done(((f32[1345,400]{1,0:T(8,128)}), f32[1345,400]{1,0:T(8,128)}) %all-reduce.5.cloned.1.call-update) | async-done | bytes 2152016 | tf_op jit(solution)/shard_map/psum | solution.py:77
  630.7 30.1 %scatter_custom_fusion.2 = f32[2048,400]{1,0:T(8,128)} fusion(s32[4096]{0:T(1024)S(1)} %bitcast.76, f32[4096,400]{1,0:T(8,128)} %bitcast.17, f32[]{:T(128)} %constant.11.clone.1), kind=kCustom, calls=%fused_computation.14 | custom fusion | flops 1638400 | bytes 3277312 | tf_op jit(solution)/shard_map/scatter-add | solution.py:86
  671.0 5.2 copy.26
  (117 shorter events, 77.4 us)
Async XLA Ops:
  9.9 19.4 %copy-start.12 = (s32[1024,2]{0,1:T(2,128)S(1)}, s32[1024,2]{0,1:T(2,128)}, u32[]{:S(2)}) copy-start(s32[1024,2]{0,1:T(2,128)} %param.9) | copy-start | bytes 24580
  38.6 19.7 %all-to-all-start = ((s32[64,1,64]{2,1,0:T(1,128)}), s32[64,1,64]{2,1,0:T(1,128)S(1)}, u32[]{:S(2)}, u32[]{:S(2)}) async-start(s32[64,1,64]{2,1,0:T(1,128)} %all_to_all.14), calls=%async_computation | async-start | bytes 65536 | tf_op jit(solution)/shard_map/all_to_all | solution.py:49
  75.7 100.4 %all-to-all-start.1 = ((bf16[64,64,400]{2,1,0:T(8,128)(2,1)}), bf16[64,64,400]{2,1,0:T(8,128)(2,1)}, u32[]{:S(2)}, u32[]{:S(2)}) async-start(bf16[64,64,400]{2,1,0:T(8,128)(2,1)} %bitcast.65), calls=%async_computation.1 | async-start | bytes 8388608 | tf_op jit(solution)/shard_map/all_to_all | solution.py:50
  83.3 22.8 %copy-start.6 = (bf16[1345,400]{0,1:T(8,128)(2,1)S(1)}, bf16[1345,400]{0,1:T(8,128)(2,1)}, u32[]{:S(2)}) copy-start(bf16[1345,400]{0,1:T(8,128)(2,1)} %param.7) | copy-start | bytes 3228004
  83.3 23.7 %copy-start.13 = (s32[1024]{0:T(1024)S(1)}, s32[1024]{0:T(1024)}, u32[]{:S(2)}) copy-start(s32[1024]{0:T(1024)} %param.10) | copy-start | bytes 12292
  84.1 21.7 %copy-start.10 = (bf16[1024,400]{0,1:T(8,128)(2,1)}, bf16[1024,400]{0,1:T(8,128)(2,1)S(1)}, u32[]{:S(2)}) copy-start(bf16[1024,400]{0,1:T(8,128)(2,1)S(1)} %constant_dynamic-slice_fusion.1) | copy-start | bytes 2457604
  84.1 21.7 %collective-permute-start = (bf16[1024,400]{0,1:T(8,128)(2,1)S(1)}, bf16[1024,400]{0,1:T(8,128)(2,1)}, u32[]{:S(2)}, u32[]{:S(2)}) collective-permute-start(bf16[1024,400]{0,1:T(8,128)(2,1)S(1)} %constant_dynamic-slice_fusion.1), channel_id=1, source_target_pairs={{0,64},{64,128},{128,192},{192,0},{1,65},{65,129},{129,193},{193,1... | collective-permute-start | bytes 2457608 | tf_op jit(solution)/shard_map/ppermute | solution.py:12
  105.8 21.0 %collective-permute-start.1 = (bf16[1024,400]{0,1:T(8,128)(2,1)}, bf16[1024,400]{0,1:T(8,128)(2,1)}, u32[]{:S(2)}, u32[]{:S(2)}) collective-permute-start(bf16[1024,400]{0,1:T(8,128)(2,1)} %collective-permute-done), channel_id=1, source_target_pairs={{0,64},{64,128},{128,192},{192,0},{1,65},{65,129},{129,193},{193,1... | collective-permute-start | bytes 2457608 | tf_op jit(solution)/shard_map/ppermute | solution.py:12
  126.8 89.9 %collective-permute-start.2 = (bf16[1024,400]{0,1:T(8,128)(2,1)}, bf16[1024,400]{0,1:T(8,128)(2,1)}, u32[]{:S(2)}, u32[]{:S(2)}) collective-permute-start(bf16[1024,400]{0,1:T(8,128)(2,1)} %collective-permute-done.1), channel_id=1, source_target_pairs={{0,64},{64,128},{128,192},{192,0},{1,65},{65,129},{129,193},{193,1... | collective-permute-start | bytes 2457608 | tf_op jit(solution)/shard_map/ppermute | solution.py:12
  205.5 11.3 %copy-start.7 = (bf16[1024,400]{0,1:T(8,128)(2,1)}, bf16[1024,400]{0,1:T(8,128)(2,1)S(1)}, u32[]{:S(2)}) copy-start(bf16[1024,400]{0,1:T(8,128)(2,1)S(1)} %fusion.11) | copy-start | bytes 2457604
  255.0 9.3 %copy-start.8 = (bf16[1024,400]{0,1:T(8,128)(2,1)S(1)}, bf16[1024,400]{0,1:T(8,128)(2,1)}, u32[]{:S(2)}) copy-start(bf16[1024,400]{0,1:T(8,128)(2,1)} %copy-done.7) | copy-start | bytes 2457604
  255.0 9.3 %copy-start.18 = (bf16[1024,1024]{1,0:T(8,128)(2,1)S(1)}, bf16[1024,1024]{1,0:T(8,128)(2,1)}, u32[]{:S(2)}) copy-start(bf16[1024,1024]{1,0:T(8,128)(2,1)} %copy-done.17) | copy-start | bytes 6291460
  255.0 375.6 %all-to-all-start.2 = ((f32[64,64,400]{2,1,0:T(8,128)}), f32[64,64,400]{2,1,0:T(8,128)}, u32[]{:S(2)}, u32[]{:S(2)}) async-start(f32[64,64,400]{2,1,0:T(8,128)} %bitcast.64), calls=%async_computation.2 | async-start | bytes 16777216 | tf_op jit(solution)/shard_map/all_to_all | solution.py:80
  264.2 167.7 %all-reduce.3.cloned.1.call-start = ((), (), s32[]{:S(2)}) async-start(), calls=%async_computation.3 | async-start | bytes 5537792 | tf_op jit(solution)/shard_map/psum | solution.py:77
  264.3 40.2 %copy-start.15 = (bf16[1024,1024]{1,0:T(8,128)(2,1)S(1)}, bf16[1024,1024]{1,0:T(8,128)(2,1)}, u32[]{:S(2)}) copy-start(bf16[1024,1024]{1,0:T(8,128)(2,1)} %copy-done.14) | copy-start | bytes 6291460
  265.3 41.7 %copy-start.2 = (f32[1024,200]{0,1:T(8,128)S(1)}, f32[1024,200]{0,1:T(8,128)}, u32[]{:S(2)}) copy-start(f32[1024,200]{0,1:T(8,128)} %get-tuple-element.4) | copy-start | bytes 2457604
  265.3 41.7 %copy-start.3 = (f32[1024,200]{0,1:T(8,128)S(1)}, f32[1024,200]{0,1:T(8,128)}, u32[]{:S(2)}) copy-start(f32[1024,200]{0,1:T(8,128)} %get-tuple-element.5) | copy-start | bytes 2457604
  265.3 39.1 %collective-permute-start.3 = (f32[1024,400]{0,1:T(8,128)S(1)}, f32[1024,400]{0,1:T(8,128)S(1)}, u32[]{:S(2)}, u32[]{:S(2)}) collective-permute-start(f32[1024,400]{0,1:T(8,128)S(1)} %fusion.21), channel_id=1, source_target_pairs={{0,64},{64,128},{128,192},{192,0},{1,65},{65,129},{129,193},{193,1... | collective-permute-start | bytes 4915208 | tf_op jit(solution)/shard_map/ppermute | solution.py:12
  306.8 52.4 %collective-permute-start.4 = (f32[1024,400]{0,1:T(8,128)}, f32[1024,400]{0,1:T(8,128)S(1)}, u32[]{:S(2)}, u32[]{:S(2)}) collective-permute-start(f32[1024,400]{0,1:T(8,128)} %convolution_add_fusion), channel_id=1, source_target_pairs={{0,64},{64,128},{128,192},{192,0},{1,65},{65,129},{129,193},{193,1... | collective-permute-start | bytes 4915208 | tf_op jit(solution)/shard_map/ppermute | solution.py:12
  309.3 9.1 %copy-start.9 = (bf16[1024,400]{0,1:T(8,128)(2,1)S(1)}, bf16[1024,400]{0,1:T(8,128)(2,1)}, u32[]{:S(2)}) copy-start(bf16[1024,400]{0,1:T(8,128)(2,1)} %copy-done.7) | copy-start | bytes 2457604
  318.3 309.1 %all-reduce.5.cloned.1.call-start = ((), (), s32[]{:S(2)}) async-start(), calls=%async_computation.4 | async-start | bytes 5537792 | tf_op jit(solution)/shard_map/psum | solution.py:77
  321.0 38.5 %copy-start.5 = (bf16[1024,1024]{1,0:T(8,128)(2,1)S(1)}, bf16[1024,1024]{1,0:T(8,128)(2,1)}, u32[]{:S(2)}) copy-start(bf16[1024,1024]{1,0:T(8,128)(2,1)} %copy-done.4) | copy-start | bytes 6291460
  359.4 56.9 %collective-permute-start.5 = (f32[1024,400]{0,1:T(8,128)S(1)}, f32[1024,400]{0,1:T(8,128)S(1)}, u32[]{:S(2)}, u32[]{:S(2)}) collective-permute-start(f32[1024,400]{0,1:T(8,128)S(1)} %add.151), channel_id=1, source_target_pairs={{0,64},{64,128},{128,192},{192,0},{1,65},{65,129},{129,193},{193,1... | collective-permute-start | bytes 4915208 | tf_op jit(solution)/shard_map/ppermute | solution.py:12
  417.8 246.3 %collective-permute-start.6 = (f32[1024,400]{0,1:T(8,128)}, f32[1024,400]{0,1:T(8,128)}, u32[]{:S(2)}, u32[]{:S(2)}) collective-permute-start(f32[1024,400]{0,1:T(8,128)} %add.152), channel_id=1, source_target_pairs={{0,64},{64,128},{128,192},{192,0},{1,65},{65,129},{129,193},{193,1... | collective-permute-start | bytes 4915208 | tf_op jit(solution)/shard_map/ppermute | solution.py:12
  (7 other events, 35.1 us)
Sparse Core Ops, SparseCore 0:
  318.4 113.4 all-reduce.2
  435.8 191.5 all-reduce.4
